TPU v7x, 32 devices: a whole 2x2x4 slice. The times are simulated.
32 devices in a mesh: pair: 8 (over z, core), orb: 4 (over y, x).
Axes of the slice: x: 2, y: 2, z: 4, core: 2. Of those that a mesh axis runs over, the one named last changes fastest.
Arguments:
- amplitudes: bfloat16 [8, 2, 600, 600], P('pair', None, 'orb'), may hold values from -6 to 6
- factors: bfloat16 [48, 360000], P('orb', 'pair'), may hold values from -0.21875 to 0.21875
- crossed_amplitudes: bfloat16 [8, 64, 600, 600], P('pair', None, 'orb'), may hold values from -6 to 6
- crossed_coupling: bfloat16 [38400, 1200], P('orb', 'pair'), may hold values from -0.03125 to 0.03125
Outputs:
- residual: float32 [8, 600, 2, 600], P('pair', 'orb')
All inputs are finite; a program needn't handle non-finite values.
Results may differ from a plain program's by a relative error of at most 0.0023.
Values may be sent and summed in bfloat16 or wider, within the bound.
No kernel may reach another device: no remote copies, remote signals or barrier semaphores. Data moves between devices by JAX's collectives and lax.ppermute only.
A program may use at most 256 MiB of HBM per device.

v0:
```python
import jax
import jax.numpy as jnp
from jax import lax
from jax.sharding import PartitionSpec as P

NV = 600


def ladder_term(amplitudes, factors, nvirt):
    pair_amps = lax.all_gather(amplitudes, "orb", axis=2, tiled=True)
    factor_rows = lax.all_gather(factors, "pair", axis=1, tiled=True)
    cube = factor_rows.reshape(factor_rows.shape[0], nvirt, nvirt)
    inner = jnp.einsum(
        "qac,jcd->jqad", cube, pair_amps[0], preferred_element_type=jnp.float32
    ).astype(jnp.bfloat16)
    return jnp.einsum("jqad,qbd->ajb", inner, cube, preferred_element_type=jnp.float32)


def crossed_term(crossed_amplitudes, crossed_coupling, nvirt):
    relaid = lax.all_to_all(crossed_amplitudes[0], "orb", split_axis=0, concat_axis=1, tiled=True)
    k_local = relaid.shape[0]
    piece = lax.all_gather(crossed_coupling, "pair", axis=1, tiled=True)
    block = piece.reshape(k_local, nvirt, piece.shape[1])
    product = jnp.einsum("kac,kcn->an", relaid, block, preferred_element_type=jnp.float32)
    return product.reshape(nvirt, product.shape[1] // nvirt, nvirt)


def on_device(amplitudes, factors, crossed_amplitudes, crossed_coupling):
    nvirt = NV
    ladder = ladder_term(amplitudes, factors, nvirt)
    crossed = crossed_term(crossed_amplitudes, crossed_coupling, nvirt)
    total = lax.psum_scatter(ladder, "orb", scatter_dimension=0, tiled=True) + lax.psum_scatter(
        crossed, "orb", scatter_dimension=0, tiled=True
    )
    return total[None]


def solution(mesh):
    return jax.shard_map(
        on_device,
        mesh=mesh,
        in_specs=(
            P("pair", None, "orb", None),
            P("orb", "pair"),
            P("pair", None, "orb", None),
            P("orb", "pair"),
        ),
        out_specs=P("pair", "orb", None, None),
        check_vma=False,
    )
```

profile of v0, /device:TPU:0, one launch (start us, length us, event | category | flops | bytes accessed | tf_op | source)
XLA Modules:
  0.0 646.5 jit_solution(15938430260463364513)
XLA Ops:
  6.5 0.0 all-gather.6.cloned.1.call-start
  6.5 0.7 all-gather.6.cloned.1.call-update
  7.3 0.0 all-gather.8.cloned.1.call-start
  7.3 0.7 all-gather.8.cloned.1.call-update
  8.0 0.0 all-gather.10.cloned.1.call-start
  8.1 0.7 all-gather.10.cloned.1.call-update
  8.7 14.3 %copy.40 = bf16[1,64,150,600]{3,2,1,0:T(8,128)(2,1)} copy(bf16[1,64,150,600]{3,1,2,0:T(8,128)(2,1)} %param.6) | data formatting | bytes 23040000 | tf_op args[2]
  23.1 6.4 all-to-all-start
  29.4 0.3 all-reduce.3.cloned.1.call-start
  29.7 87.7 %all-gather.6.cloned.1.call-done = bf16[1,2,600,600]{3,1,0,2:T(2,128)(2,1)} async-done(((bf16[1,2,150,600]{3,1,0,2:T(2,128)(2,1)}), bf16[1,2,600,600]{3,1,0,2:T(2,128)(2,1)}) %all-gather.6.cloned.1.call-update) | async-done | bytes 1440016 | tf_op jit(solution)/shard_map/all_gather | solution.py:10
  117.4 3.8 copy.19
  121.2 53.8 %all-to-all-done = bf16[64,150,600]{2,1,0:T(8,128)(2,1)} async-done(((bf16[64,150,600]{2,1,0:T(8,128)(2,1)}), bf16[64,150,600]{2,1,0:T(8,128)(2,1)}, u32[]{:S(2)}, u32[]{:S(2)}) %all-to-all-start) | async-done | bytes 11520032 | tf_op jit(solution)/shard_map/all_to_all | solution.py:20
  175.0 27.9 %copy.24 = bf16[16,4,150,600]{3,0,2,1:T(8,128)(2,1)} copy(bf16[16,4,150,600]{3,2,0,1:T(8,128)(2,1)} %bitcast.14) | data formatting | bytes 23040000 | tf_op jit(solution)/shard_map/all_to_all | solution.py:20
  202.9 23.4 %all-gather.8.cloned.1.call-done = bf16[8,45000,12]{1,2,0:T(8,128)(2,1)} async-done(((bf16[1,45000,12]{1,2,0:T(8,128)(2,1)}), bf16[8,45000,12]{1,2,0:T(8,128)(2,1)}) %all-gather.8.cloned.1.call-update) | async-done | bytes 8640016 | tf_op jit(solution)/shard_map/all_gather | solution.py:11
  226.4 13.7 %copy.20 = bf16[8,45000,12]{1,0,2:T(8,128)(2,1)} copy(bf16[8,45000,12]{1,2,0:T(8,128)(2,1)} %all-gather.8.cloned.1.call-done) | data formatting | bytes 17280000 | tf_op jit(solution)/shard_map/all_gather | solution.py:11
  240.1 34.1 %reshape.11 = bf16[360000,12]{0,1:T(8,128)(2,1)} reshape(bf16[8,45000,12]{1,0,2:T(8,128)(2,1)} %copy.20) | data formatting | bytes 17280000
  274.2 23.4 %reshape.15 = bf16[12,600,600,1]{2,1,0,3:T(8,128)(2,1)} reshape(bf16[12,360000]{1,0:T(8,128)(2,1)} %bitcast.66) | data formatting | bytes 17280000 | tf_op jit(solution)/shard_map/reshape | solution.py:12
  297.7 21.1 %fusion.24 = bf16[2,12,600,600]{2,3,1,0:T(8,128)(2,1)} fusion(bf16[12,600,600,1]{2,1,0,3:T(8,128)(2,1)} %reshape.15, bf16[1,2,600,600]{2,3,1,0:T(8,128)(2,1)S(1)} %copy.19), kind=kOutput, calls=%fused_computation.3.clone.clone.clone.1 | convolution fusion | flops 10376640512 | bytes 27360000 | tf_op jit(solution)/shard_map/qac,jcd->jqad/dot_general | solution.py:13
  318.8 112.4 %all-gather.10.cloned.1.call-done = bf16[8,150,9600]{2,1,0:T(8,128)(2,1)} async-done(((bf16[1,150,9600]{2,1,0:T(8,128)(2,1)}), bf16[8,150,9600]{2,1,0:T(8,128)(2,1)}) %all-gather.10.cloned.1.call-update) | async-done | bytes 23040016 | tf_op jit(solution)/shard_map/all_gather | solution.py:22
  431.2 24.2 %reshape.13 = bf16[1200,9600]{1,0:T(8,128)(2,1)} reshape(bf16[8,150,9600]{2,1,0:T(8,128)(2,1)} %all-gather.10.cloned.1.call-done) | data formatting | bytes 46080000
  455.4 49.1 %reshape.9 = bf16[16,600,1200]{1,0,2:T(8,128)(2,1)} reshape(bf16[9600,1200]{0,1:T(8,128)(2,1)} %bitcast.64) | data formatting | bytes 46080000 | tf_op jit(solution)/shard_map/reshape | solution.py:23
  504.5 24.8 %fusion = f32[600,2,600,1]{2,0,3,1:T(8,128)S(1)} fusion(bf16[2,600,600,16]{2,3,1,0:T(8,128)(2,1)} %bitcast.67, bf16[16,600,600]{2,0,1:T(8,128)(2,1)} %bitcast.68), kind=kOutput, calls=%fused_computation | convolution fusion | flops 13824000000 | bytes 37440000 | tf_op jit(solution)/shard_map/kac,kcn->an/dot_general | solution.py:24
  529.3 20.6 %bitcast_add_fusion = f32[600,2,600]{2,0,1:T(8,128)S(1)} fusion(f32[600,2,600,1]{2,0,3,1:T(8,128)S(1)} %fusion, bf16[12,600,600,1]{2,1,0,3:T(8,128)(2,1)} %reshape.15, bf16[2,12,600,600]{2,3,1,0:T(8,128)(2,1)} %fusion.24), kind=kOutput, calls=%fused_computation.8 | convolution fusion | flops 10368719872 | bytes 31680000 | tf_op jit(solution)/shard_map/jqad,qbd->ajb/dot_general | solution.py:16
  549.9 0.0 copy-start
  549.9 3.2 copy.27
  553.1 0.0 all-reduce.3.cloned.1.call-update
  553.1 0.0 copy-done
  553.1 0.6 dynamic-slice
  554.4 82.9 %all-reduce.3.cloned.1.call-done = f32[600,2,600]{2,1,0:T(2,128)} async-done(((f32[600,2,600]{2,1,0:T(2,128)}), f32[600,2,600]{2,1,0:T(2,128)}) %all-reduce.3.cloned.1.call-update) | async-done | bytes 2880016
  637.2 2.3 dynamic-slice_bitcast_fusion
Async XLA Ops:
  6.5 110.9 %all-gather.6.cloned.1.call-start = ((), (), s32[]{:S(2)}) async-start(), calls=%async_computation.1 | async-start | bytes 1920000 | tf_op jit(solution)/shard_map/all_gather | solution.py:10
  7.3 219.1 %all-gather.8.cloned.1.call-start = ((), (), s32[]{:S(2)}) async-start(), calls=%async_computation.2 | async-start | bytes 12976128 | tf_op jit(solution)/shard_map/all_gather | solution.py:11
  8.0 423.2 %all-gather.10.cloned.1.call-start = ((), (), s32[]{:S(2)}) async-start(), calls=%async_computation.3 | async-start | bytes 26265600 | tf_op jit(solution)/shard_map/all_gather | solution.py:22
  23.1 151.9 %all-to-all-start = ((bf16[64,150,600]{2,1,0:T(8,128)(2,1)}), bf16[64,150,600]{2,1,0:T(8,128)(2,1)}, u32[]{:S(2)}, u32[]{:S(2)}) async-start(bf16[64,150,600]{2,1,0:T(8,128)(2,1)} %bitcast.65), calls=%async_computation | async-start | bytes 24903680 | tf_op jit(solution)/shard_map/all_to_all | solution.py:20
  29.4 607.8 %all-reduce.3.cloned.1.call-start = ((), (), s32[]{:S(2)}) async-start(), calls=%async_computation.4 | async-start | bytes 6144000
  549.9 3.3 copy-start
Sparse Core Ops, SparseCore 0:
  9.2 108.2 all-gather.5
  119.1 107.2 all-gather.7
  228.0 203.1 all-gather.9
  553.2 83.9 all-reduce.2
where the time goes:
time: 651 us; the launch traced here: 646 us
  waiting for transfers between devices  362 us (56%)
  local copies, waits for them, and re-layouts  197 us (30%)
  matrix products  66.5 us (10%)
  between operations  14.3 us (2%)
  starting transfers between devices  6.7 us (1%)
    all_gather x1, waiting for transfers between devices, crossed_term(): piece = lax.all_gather(crossed_coupling, 'pair', axis=1, tiled=True)  112 us
    all_gather x1, waiting for transfers between devices, ladder_term(): pair_amps = lax.all_gather(amplitudes, 'orb', axis=2, tiled=True)  87.7 us
    unnamed x5, waiting for transfers between devices  85 us
    unnamed x6, local copies, waits for them, and re-layouts  73.2 us
    all_to_all x1, waiting for transfers between devices, crossed_term(): lax.all_to_all(crossed_amplitudes[0], 'orb', split_axis=0, concat_axis=1,...  53.8 us
    reshape x1, local copies, waits for them, and re-layouts, crossed_term(): block = piece.reshape(k_local, nvirt, piece.shape[1])  49.1 us
    all_to_all x1, local copies, waits for them, and re-layouts, crossed_term(): lax.all_to_all(crossed_amplitudes[0], 'orb', split_axis=0, concat_axis=1,...  27.9 us
    dot_general x1, matrix products, crossed_term(): jnp.einsum('kac,kcn->an', relaid, block, preferred_element_type=jnp.float32)  24.8 us
  transfers between devices with their start and end apart: 5, of which 5 were waited for; matrix products, arithmetic and copies ran while one was open for 22% of the time, Pallas kernels for 0%

commit v1 on v0

--- a/solution.py
+++ b/solution.py
@@ -7,7 +7,18 @@
 
 
 def ladder_term(amplitudes, factors, nvirt):
-    pair_amps = lax.all_gather(amplitudes, "orb", axis=2, tiled=True)
+    mid_arr = lax.axis_index("orb")
+    tmp = lax.axis_size("orb")
+    small, v1 = (tmp, mid_arr)
+    pair_amps, d_next = (amplitudes, 1)
+    while d_next < small:
+        part_next = lax.ppermute(
+            pair_amps, axis_name="orb", perm=[(i, i ^ d_next) for i in range(small)]
+        )
+        heard = jnp.concatenate([pair_amps, part_next], axis=2)
+        part_now = jnp.concatenate([part_next, pair_amps], axis=2)
+        pair_amps = jnp.where(v1 & d_next == 0, heard, part_now)
+        d_next = 2 * d_next
     factor_rows = lax.all_gather(factors, "pair", axis=1, tiled=True)
     cube = factor_rows.reshape(factor_rows.shape[0], nvirt, nvirt)
     inner = jnp.einsum(

time: 651 us -> 544 us (0.84)
  waiting for transfers between devices: 362 us -> 242 us
  other arithmetic: 0 us -> 15.2 us
    ppermute x0 -> x2, waiting for transfers between devices: none -> 155 us  [ladder_term(): lax.ppermute(pair_amps, axis_name='orb', perm=[(i, i ^ d_next) for i in r...]
    all_gather x1, waiting for transfers between devices: 112 us -> 2.65 us  [crossed_term(): piece = lax.all_gather(crossed_coupling, 'pair', axis=1, tiled=True)]
    all_gather x1 -> x0, waiting for transfers between devices: 87.7 us -> none  [ladder_term(): pair_amps = lax.all_gather(amplitudes, 'orb', axis=2, tiled=True)]
    all_to_all x1, waiting for transfers between devices: 53.8 us -> 0.01 us  [crossed_term(): lax.all_to_all(crossed_amplitudes[0], 'orb', split_axis=0, concat_axis=1,...]
    all_gather x1, waiting for transfers between devices: 23.4 us -> 0.02 us  [ladder_term(): factor_rows = lax.all_gather(factors, 'pair', axis=1, tiled=True)]
    select_n x0 -> x3, other arithmetic: none -> 15.2 us  [ladder_term(): pair_amps = jnp.where(v1 & d_next == 0, heard, part_now)]
    unnamed x5 -> x4, waiting for transfers between devices: 85 us -> 84.3 us
    unnamed x6 -> x8, local copies, waits for them, and re-layouts: 73.2 us -> 72.6 us
  transfers between devices with their start and end apart: 5 -> 6, of which waited for: 5 -> 4; matrix products, arithmetic and copies ran while one was open for 22% -> 27% of each run, Pallas kernels for 0% -> 0%
where the time goes in v1:
time: 544 us; the launch traced here: 540 us
  waiting for transfers between devices  242 us (44%)
  local copies, waits for them, and re-layouts  191 us (35%)
  matrix products  65.3 us (12%)
  other arithmetic  15.2 us (3%)
  between operations  14.3 us (3%)
  starting transfers between devices  11.3 us (2%)
    ppermute x2, waiting for transfers between devices, ladder_term(): lax.ppermute(pair_amps, axis_name='orb', perm=[(i, i ^ d_next) for i in r...  155 us
    unnamed x4, waiting for transfers between devices  84.3 us
    unnamed x8, local copies, waits for them, and re-layouts  72.6 us
    reshape x1, local copies, waits for them, and re-layouts, crossed_term(): block = piece.reshape(k_local, nvirt, piece.shape[1])  49.1 us
    all_to_all x1, local copies, waits for them, and re-layouts, crossed_term(): lax.all_to_all(crossed_amplitudes[0], 'orb', split_axis=0, concat_axis=1,...  28.5 us
    dot_general x1, matrix products, crossed_term(): jnp.einsum('kac,kcn->an', relaid, block, preferred_element_type=jnp.float32)  24.8 us
    reshape x1, local copies, waits for them, and re-layouts, ladder_term(): cube = factor_rows.reshape(factor_rows.shape[0], nvirt, nvirt)  23.2 us
    dot_general x1, matrix products, ladder_term(): jnp.einsum('jqad,qbd->ajb', inner, cube, preferred_element_type=jnp.float32)  20.6 us
  transfers between devices with their start and end apart: 6, of which 4 were waited for; matrix products, arithmetic and copies ran while one was open for 27% of the time, Pallas kernels for 0%

profile of v1, /device:TPU:0, one launch (start us, length us, event | category | flops | bytes accessed | tf_op | source)
XLA Modules:
  0.0 539.9 jit_solution(15371621985668945203)
XLA Ops:
  6.5 0.0 all-gather.5.cloned.1.call-start
  6.5 0.7 all-gather.5.cloned.1.call-update
  7.3 0.0 all-gather.7.cloned.1.call-start
  7.3 0.7 all-gather.7.cloned.1.call-update
  8.0 14.4 %copy.47 = bf16[1,64,150,600]{3,2,1,0:T(8,128)(2,1)} copy(bf16[1,64,150,600]{3,1,2,0:T(8,128)(2,1)} %param.6) | data formatting | bytes 23040000 | tf_op args[2]
  22.4 0.0 copy-start
  22.4 6.5 %all-to-all-start = ((bf16[64,150,600]{2,1,0:T(8,128)(2,1)}), bf16[64,150,600]{2,1,0:T(8,128)(2,1)}, u32[]{:S(2)}, u32[]{:S(2)}) async-start(bf16[64,150,600]{2,1,0:T(8,128)(2,1)} %bitcast.59), calls=%async_computation | async-start | bytes 24903680 | tf_op jit(solution)/shard_map/all_to_all | solution.py:31
  28.9 0.3 all-reduce.3.cloned.1.call-start
  29.2 0.0 copy-done
  29.2 3.0 collective-permute-start
  32.2 142.2 %collective-permute-done = bf16[1,2,150,600]{3,1,2,0:T(2,128)(2,1)S(1)} collective-permute-done((bf16[1,2,150,600]{3,1,2,0:T(2,128)(2,1)S(1)}, bf16[1,2,150,600]{3,1,2,0:T(2,128)(2,1)S(1)}, u32[]{:S(2)}, u32[]{:S(2)}) %collective-permute-start) | collective-permute-done | bytes 360032 | tf_op jit(solution)/shard_map/ppermute | solution.py:15
  174.4 3.8 broadcast_select_fusion.1
  178.2 1.5 collective-permute-start.1
  179.7 3.8 broadcast_select_fusion.2
  183.6 13.1 %collective-permute-done.1 = bf16[1,2,300,600]{3,1,2,0:T(2,128)(2,1)S(1)} collective-permute-done((bf16[1,2,300,600]{3,1,2,0:T(2,128)(2,1)S(1)}, bf16[1,2,300,600]{3,1,2,0:T(2,128)(2,1)S(1)}, u32[]{:S(2)}, u32[]{:S(2)}) %collective-permute-start.1) | collective-permute-done | bytes 720032 | tf_op jit(solution)/shard_map/ppermute | solution.py:15
  196.7 7.6 %fusion.11 = bf16[2,600,600,1]{2,0,1,3:T(2,128)(2,1)S(1)} fusion(pred[]{:T(512)S(6)} %eq.6, bf16[2,300,600]{2,0,1:T(2,128)(2,1)S(1)} %bitcast.67, bf16[2,300,600]{2,0,1:T(2,128)(2,1)S(1)} %broadcast_select_fusion.2), kind=kLoop, calls=%fused_computation.11 | loop fusion | flops 2160000 | bytes 2880001 | tf_op jit(solution)/shard_map/jit(_where)/select_n | solution.py:20
  204.3 0.0 all-to-all-done
  204.3 28.5 %copy.23 = bf16[16,4,150,600]{3,0,2,1:T(8,128)(2,1)} copy(bf16[16,4,150,600]{3,2,0,1:T(8,128)(2,1)} %bitcast.14) | data formatting | bytes 23040000 | tf_op jit(solution)/shard_map/all_to_all | solution.py:31
  232.8 0.0 all-gather.5.cloned.1.call-done
  232.8 12.6 %copy.18 = bf16[8,45000,12]{1,0,2:T(8,128)(2,1)} copy(bf16[8,45000,12]{1,2,0:T(8,128)(2,1)} %all-gather.5.cloned.1.call-done) | data formatting | bytes 17280000 | tf_op jit(solution)/shard_map/all_gather | solution.py:22
  245.3 33.4 %reshape.94 = bf16[360000,12]{0,1:T(8,128)(2,1)} reshape(bf16[8,45000,12]{1,0,2:T(8,128)(2,1)} %copy.18) | data formatting | bytes 17280000
  278.8 23.2 %reshape.98 = bf16[12,600,600,1]{2,1,0,3:T(8,128)(2,1)} reshape(bf16[12,360000]{1,0:T(8,128)(2,1)} %bitcast.60) | data formatting | bytes 17280000 | tf_op jit(solution)/shard_map/reshape | solution.py:23
  302.0 20.0 %fusion.25 = bf16[2,12,600,600]{2,3,1,0:T(8,128)(2,1)} fusion(bf16[12,600,600,1]{2,1,0,3:T(8,128)(2,1)} %reshape.98, bf16[2,600,600,1]{2,0,1,3:T(2,128)(2,1)S(1)} %fusion.11), kind=kOutput, calls=%fused_computation.3.clone.clone.clone.1 | convolution fusion | flops 10376640512 | bytes 27360000 | tf_op jit(solution)/shard_map/qac,jcd->jqad/dot_general | solution.py:24
  322.0 2.7 all-gather.7.cloned.1.call-done
  324.6 24.2 %reshape.96 = bf16[1200,9600]{1,0:T(8,128)(2,1)} reshape(bf16[8,150,9600]{2,1,0:T(8,128)(2,1)} %all-gather.7.cloned.1.call-done) | data formatting | bytes 46080000
  348.8 49.1 %reshape.92 = bf16[16,600,1200]{1,0,2:T(8,128)(2,1)} reshape(bf16[9600,1200]{0,1:T(8,128)(2,1)} %bitcast.58) | data formatting | bytes 46080000 | tf_op jit(solution)/shard_map/reshape | solution.py:34
  397.9 24.8 %fusion = f32[600,2,600,1]{2,0,3,1:T(8,128)S(1)} fusion(bf16[2,600,600,16]{2,3,1,0:T(8,128)(2,1)} %bitcast.61, bf16[16,600,600]{2,0,1:T(8,128)(2,1)} %bitcast.62), kind=kOutput, calls=%fused_computation | convolution fusion | flops 13824000000 | bytes 37440000 | tf_op jit(solution)/shard_map/kac,kcn->an/dot_general | solution.py:35
  422.7 20.6 %bitcast_add_fusion = f32[600,2,600]{2,0,1:T(8,128)S(1)} fusion(f32[600,2,600,1]{2,0,3,1:T(8,128)S(1)} %fusion, bf16[12,600,600,1]{2,1,0,3:T(8,128)(2,1)} %reshape.98, bf16[2,12,600,600]{2,3,1,0:T(8,128)(2,1)} %fusion.25), kind=kOutput, calls=%fused_computation.8 | convolution fusion | flops 10368719872 | bytes 31680000 | tf_op jit(solution)/shard_map/jqad,qbd->ajb/dot_general | solution.py:27
  443.3 0.0 copy-start.1
  443.3 3.2 copy.26
  446.5 0.0 all-reduce.3.cloned.1.call-update
  446.5 0.0 copy-done.1
  446.6 0.6 dynamic-slice
  447.8 82.9 %all-reduce.3.cloned.1.call-done = f32[600,2,600]{2,1,0:T(2,128)} async-done(((f32[600,2,600]{2,1,0:T(2,128)}), f32[600,2,600]{2,1,0:T(2,128)}) %all-reduce.3.cloned.1.call-update) | async-done | bytes 2880016
  530.7 2.3 dynamic-slice_bitcast_fusion
Async XLA Ops:
  6.5 226.2 %all-gather.5.cloned.1.call-start = ((), (), s32[]{:S(2)}) async-start(), calls=%async_computation.1 | async-start | bytes 12976128 | tf_op jit(solution)/shard_map/all_gather | solution.py:22
  7.3 317.4 %all-gather.7.cloned.1.call-start = ((), (), s32[]{:S(2)}) async-start(), calls=%async_computation.2 | async-start | bytes 26265600 | tf_op jit(solution)/shard_map/all_gather | solution.py:33
  22.4 6.8 %copy-start = (bf16[1,2,150,600]{3,1,2,0:T(2,128)(2,1)S(1)}, bf16[1,2,150,600]{3,1,2,0:T(2,128)(2,1)}, u32[]{:S(2)}) copy-start(bf16[1,2,150,600]{3,1,2,0:T(2,128)(2,1)} %param.4) | copy-start | bytes 1080004
  22.4 181.9 %all-to-all-start = ((bf16[64,150,600]{2,1,0:T(8,128)(2,1)}), bf16[64,150,600]{2,1,0:T(8,128)(2,1)}, u32[]{:S(2)}, u32[]{:S(2)}) async-start(bf16[64,150,600]{2,1,0:T(8,128)(2,1)} %bitcast.59), calls=%async_computation | async-start | bytes 24903680 | tf_op jit(solution)/shard_map/all_to_all | solution.py:31
  28.9 501.8 %all-reduce.3.cloned.1.call-start = ((), (), s32[]{:S(2)}) async-start(), calls=%async_computation.3 | async-start | bytes 6144000
  29.2 145.2 %collective-permute-start = (bf16[1,2,150,600]{3,1,2,0:T(2,128)(2,1)S(1)}, bf16[1,2,150,600]{3,1,2,0:T(2,128)(2,1)S(1)}, u32[]{:S(2)}, u32[]{:S(2)}) collective-permute-start(bf16[1,2,150,600]{3,1,2,0:T(2,128)(2,1)S(1)} %copy-done), channel_id=1, source_target_pairs={{0,1},{1,0},{2,3},{3,2},{4,5},{5,4},{6,7},{7,6},{8,9},{9,8},{10,11... | collective-permute-start | bytes 1080008 | tf_op jit(solution)/shard_map/ppermute | solution.py:15
  178.2 18.5 %collective-permute-start.1 = (bf16[1,2,300,600]{3,1,2,0:T(2,128)(2,1)S(1)}, bf16[1,2,300,600]{3,1,2,0:T(2,128)(2,1)S(1)}, u32[]{:S(2)}, u32[]{:S(2)}) collective-permute-start(bf16[1,2,300,600]{3,1,2,0:T(2,128)(2,1)S(1)} %broadcast_select_fusion.1), channel_id=1, source_target_pairs={{0,2},{1,3},{2,0},{3,1},{4,6},{5,7},{6,4},{7,5},{8,10},{9,11},{10,... | collective-permute-start | bytes 2160008 | tf_op jit(solution)/shard_map/ppermute | solution.py:15
  443.3 3.3 copy-start.1
Sparse Core Ops, SparseCore 0:
  9.0 110.7 all-gather.4
  121.4 203.1 all-gather.6
  446.7 83.9 all-reduce.2
